TPU v7x, 512 devices: a whole 4x4x16 slice. The times are simulated.
512 devices in a mesh: dp: 4 (over z_hi, core), tm: 8 (over z_lo), height: 16 (over x, y).
Axes of the slice: x: 4, y: 4, z: 16 (z_hi: 2, z_lo: 8; z = z_hi * 8 + z_lo), core: 2. Of those that a mesh axis runs over, the one named last changes fastest.
Arguments:
- clips: bfloat16 [4, 16, 64, 128, 128], P('dp', 'tm', 'height'), may hold values from -6 to 6
- frame_counts: int32 [4, 5], P('dp'), may hold values from 1 to 9, 16 in all within a row
- conv_first: bfloat16 [3, 3, 3, 128, 128], replicated, may hold values from -0.109375 to 0.109375
- conv_down: bfloat16 [3, 3, 3, 128, 128], replicated, may hold values from -0.109375 to 0.109375
- out_cotangent: bfloat16 [4, 8, 32, 64, 128], P('dp', 'tm', 'height'), may hold values from -6 to 6
Outputs:
- encoded: bfloat16 [4, 8, 32, 64, 128], P('dp', 'tm', 'height')
- grad_first: bfloat16 [3, 3, 3, 128, 128], P(None, None, None, 'dp')
- grad_down: bfloat16 [3, 3, 3, 128, 128], P(None, None, None, 'dp')
Inputs may be any that keep to these rules, and one draw needn't show every extreme that they name: `frame_counts`: each sequence's 5 clip lengths sum to 16; in every sequence one clip has exactly 9 frames.
All inputs are finite; a program needn't handle non-finite values.
Results may differ from a plain program's by a relative error of at most 0.0059.
Values may be sent and summed in bfloat16 or wider, within the bound.
No kernel may reach another device: no remote copies, remote signals or barrier semaphores. Data moves between devices by JAX's collectives and lax.ppermute only.
A program may use at most 64 MiB of HBM per device.

v0:
```python
import math
import jax
import jax.numpy as jnp
from jax import lax
from jax.sharding import PartitionSpec as P


def padded_2(cells, sides, width):
    for axis, dim in sides:
        count = lax.axis_size(axis)
        ends = count - 1
        head = lax.slice_in_dim(cells, 0, width, axis=dim)
        tail = lax.slice_in_dim(cells, cells.shape[dim] - width, cells.shape[dim], axis=dim)
        cells = jnp.concatenate(
            [
                lax.ppermute(tail, axis, [(i, (i + 1) % count) for i in range(ends)]),
                cells,
                lax.ppermute(head, axis, [((i + 1) % count, i) for i in range(ends)]),
            ],
            axis=dim,
        )
    return cells


def shifted(value, axis, steps):
    count = lax.axis_size(axis)
    leading, last = (max(0, -steps), min(count, count - steps))
    return lax.ppermute(value, axis, [(source, source + steps) for source in range(leading, last)])


def unfold(frame_slab, stride, pad_cols):
    padded = jnp.pad(frame_slab, ((0, 0), (0, 0), pad_cols, (0, 0)))
    out_rows = (padded.shape[1] - 3) // stride + 1
    out_cols = (padded.shape[2] - 3) // stride + 1
    pieces = []
    for tap_row in range(3):
        for tap_col in range(3):
            pieces.append(
                padded[
                    :,
                    tap_row : tap_row + stride * (out_rows - 1) + 1 : stride,
                    tap_col : tap_col + stride * (out_cols - 1) + 1 : stride,
                ]
            )
    joined = jnp.concatenate(pieces, axis=-1)
    return (joined.reshape(-1, joined.shape[-1]), (frame_slab.shape[0], out_rows, out_cols))


def conv_layer(extended, weight, tap_mask, out_frames, stride, pad_cols):
    channels_out = weight.shape[-1]
    summed = None
    for tap_time in range(3):
        frame_slab = extended[tap_time : tap_time + stride * (out_frames - 1) + 1 : stride]
        columns, shape_out = unfold(frame_slab, stride, pad_cols)
        kernel = weight[tap_time].reshape(-1, channels_out)
        tap_term = jnp.dot(columns, kernel, preferred_element_type=jnp.float32).reshape(
            shape_out + (channels_out,)
        )
        tap_term = tap_term * tap_mask[:, tap_time][:, None, None, None]
        summed = tap_term if summed is None else summed + tap_term
    return summed


def weight_grad(extended, grads, tap_mask, stride, pad_cols):
    out_frames = grads.shape[0]
    blocks = []
    for tap_time in range(3):
        frame_slab = extended[tap_time : tap_time + stride * (out_frames - 1) + 1 : stride]
        columns, shape_out = unfold(frame_slab, stride, pad_cols)
        masked = grads * tap_mask[:, tap_time].astype(jnp.bfloat16)[:, None, None, None]
        blocks.append(
            jnp.dot(
                columns.T, masked.reshape(-1, grads.shape[-1]), preferred_element_type=jnp.float32
            )
        )
    stacked = jnp.stack(blocks)
    return stacked.reshape(3, 3, 3, extended.shape[-1], grads.shape[-1])


def hidden_grad(grads_ext, weight, mask_ext):
    pieces = []
    for tap_time in range(3):
        masked = grads_ext * mask_ext[:, tap_time].astype(jnp.bfloat16)[:, None, None, None]
        kernel = jnp.transpose(weight[tap_time][::-1, ::-1], (0, 1, 3, 2))
        spread = lax.conv_general_dilated(
            masked,
            kernel,
            (1, 1),
            ((2, 0), (2, 2)),
            lhs_dilation=(2, 2),
            dimension_numbers=("NHWC", "HWIO", "NHWC"),
            preferred_element_type=jnp.float32,
        )
        pieces.append(spread[:, 1:, 1:])
    even_frames = pieces[2][:-1] + pieces[0][1:]
    odd_frames = pieces[1][1:]
    merged = jnp.stack([even_frames, odd_frames], axis=1)
    return merged.reshape((2 * even_frames.shape[0],) + even_frames.shape[1:])


def positions(counts_row, frame_index):
    starts = jnp.cumsum(counts_row) - counts_row
    latest = jnp.max(jnp.where(starts[None, :] <= frame_index[:, None], starts[None, :], 0), axis=1)
    return frame_index - latest


def tap_masks(place):
    return (place[:, None] >= (2 - jnp.arange(3, dtype=jnp.int32))[None, :]).astype(jnp.float32)


def body(clips, frame_counts, conv_first, conv_down, out_cotangent):
    frames_dev = clips.shape[1]
    rows_dev = clips.shape[2]
    columns_all = clips.shape[3]
    down_frames = frames_dev // 2
    counts_row = frame_counts[0]
    first_frame = lax.axis_index("tm") * frames_dev
    frame_index = first_frame + jnp.arange(frames_dev, dtype=jnp.int32)
    first_mask = tap_masks(positions(counts_row, frame_index))
    down_index = first_frame + 2 * jnp.arange(down_frames + 1, dtype=jnp.int32)
    mask_ext = tap_masks(positions(counts_row, down_index))
    down_mask = mask_ext[:down_frames]
    with_rows = padded_2(clips[0], (("height", 1),), 1)
    earlier = shifted(with_rows, "tm", 1)
    input_ext = jnp.concatenate([earlier, with_rows], axis=0)
    pre_act = conv_layer(input_ext, conv_first, first_mask, frames_dev, 1, (1, 1))
    hidden = jax.nn.silu(pre_act).astype(jnp.bfloat16)
    above = shifted(hidden[:, rows_dev - 1 :], "height", 1)
    hidden_rows = jnp.concatenate([above, hidden], axis=1)
    hidden_past = shifted(hidden_rows, "tm", 1)
    hidden_ext = jnp.concatenate([hidden_past, hidden_rows], axis=0)
    encoded = conv_layer(hidden_ext, conv_down, down_mask, down_frames, 2, (1, 0)).astype(
        jnp.bfloat16
    )
    cells_all = (
        lax.axis_size("dp")
        * clips.shape[0]
        * down_frames
        * lax.axis_size("tm")
        * (rows_dev // 2)
        * lax.axis_size("height")
        * (columns_all // 2)
    )
    scale = 1.0 / math.sqrt(cells_all)
    grads = (out_cotangent[0].astype(jnp.float32) * scale).astype(jnp.bfloat16)
    down_local = weight_grad(hidden_ext, grads, down_mask, 2, (1, 0))
    below = shifted(grads[:, 0:1], "height", -1)
    grads_rows = jnp.concatenate([grads, below], axis=1)
    grads_next = shifted(grads_rows, "tm", -1)
    grads_ext = jnp.concatenate([grads_rows, grads_next], axis=0)
    back_hidden = hidden_grad(grads_ext, conv_down, mask_ext).astype(jnp.bfloat16)
    sigma = jax.nn.sigmoid(pre_act)
    pre_grad = (back_hidden.astype(jnp.float32) * sigma * (1.0 + pre_act * (1.0 - sigma))).astype(
        jnp.bfloat16
    )
    first_local = weight_grad(input_ext, pre_grad, first_mask, 1, (1, 1))
    share = conv_first.shape[3] // lax.axis_size("dp")
    quarters = lax.axis_size("dp")

    def by_quarter(term):
        term = term.reshape(27, quarters, share, term.shape[-1])
        return jnp.transpose(term, (1, 0, 2, 3)).reshape(quarters, -1)

    stacked = jnp.concatenate([by_quarter(first_local), by_quarter(down_local)], axis=1)
    rows_n, frames_n = (lax.axis_size("height"), lax.axis_size("tm"))
    piece = stacked.reshape(quarters, rows_n, frames_n, -1)
    piece = lax.psum_scatter(piece, "height", scatter_dimension=1, tiled=True)
    piece = lax.psum_scatter(piece, "tm", scatter_dimension=2, tiled=True)
    piece = lax.psum_scatter(piece, "dp", scatter_dimension=0, tiled=True)
    piece = piece.astype(jnp.bfloat16)
    piece = lax.all_gather(piece, "tm", axis=2, tiled=True)
    gathered = lax.all_gather(piece, "height", axis=1, tiled=True).reshape(-1)
    half = gathered.shape[0] // 2
    kernel_shape = (3, 3, 3, share, conv_first.shape[-1])
    summed_first = gathered[:half].reshape(kernel_shape)
    summed_down = gathered[half:].reshape(kernel_shape)
    return (encoded[None], summed_first, summed_down)


def solution(mesh):
    in_specs = (
        P("dp", "tm", "height", None, None),
        P("dp", None),
        P(),
        P(),
        P("dp", "tm", "height", None, None),
    )
    out_specs = (
        P("dp", "tm", "height", None, None),
        P(None, None, None, "dp", None),
        P(None, None, None, "dp", None),
    )
    return jax.shard_map(body, mesh=mesh, in_specs=in_specs, out_specs=out_specs, check_vma=False)
```

profile of v0, /device:TPU:32, one launch (start us, length us, event | category | flops | bytes accessed | tf_op | source)
XLA Modules:
  0.0 460.8 jit_solution(5492218654866860973)
XLA Ops:
  7.2 0.9 fusion.92
  8.1 3.5 collective-permute-start
  11.6 1.3 collective-permute-start.1
  12.9 0.8 fusion.60
  13.7 1.3 collective-permute-start.5
  15.0 0.8 reduce-window_clone.1
  15.9 0.7 subtract_bitcast_fusion
  16.9 1.2 fusion.89
  21.7 5.2 %collective-permute-start.6 = (bf16[1,3,64,128]{3,2,1,0:T(8,128)(2,1)S(1)}, bf16[1,3,64,128]{3,2,1,0:T(8,128)(2,1)S(1)}, u32[]{:S(2)}, u32[]{:S(2)}) collective-permute-start(bf16[1,3,64,128]{3,2,1,0:T(8,128)(2,1)S(1)} %pad_maximum_fusion.8), channel_id=1, source_target_pairs={{16,0},{32,16},{48,32},{64,48},{80,64},{96,80},{112,96},{17,1},{33... | collective-permute-start | bytes 147464 | tf_op jit(solution)/shard_map/ppermute | solution.py:28
  27.0 2.1 collective-permute-start.2
  29.2 1.3 multiply_bitcast_fusion.1
  33.1 3.8 collective-permute-done.2
  37.9 0.8 convolution_multiply_fusion.1
  39.6 0.8 fusion.1
  40.4 0.9 fusion.10
  41.3 0.9 convolution_bitcast_fusion.5
  42.2 0.9 convolution_bitcast_fusion.4
  43.0 0.9 convolution_bitcast_fusion.3
  43.9 5.2 %collective-permute-start.3 = (bf16[2,1,128,128]{3,2,1,0:T(8,128)(2,1)S(1)}, bf16[2,1,128,128]{3,2,1,0:T(8,128)(2,1)S(1)}, u32[]{:S(2)}, u32[]{:S(2)}) collective-permute-start(bf16[2,1,128,128]{3,2,1,0:T(8,128)(2,1)S(1)} %slice.447), channel_id=1, source_target_pairs={{0,1},{1,2},{2,3},{3,4},{4,5},{5,6},{6,7},{7,8},{8,9},{9,10},{10,1... | collective-permute-start | bytes 196616 | tf_op jit(solution)/shard_map/ppermute | solution.py:28
  49.2 1.4 copy.96
  50.6 1.9 concatenate.66
  53.9 3.2 collective-permute-start.4
  57.5 5.3 %collective-permute-done.4 = bf16[2,5,128,128]{3,2,1,0:T(8,128)(2,1)S(1)} collective-permute-done((bf16[2,5,128,128]{3,2,1,0:T(8,128)(2,1)S(1)}, bf16[2,5,128,128]{3,2,1,0:T(8,128)(2,1)S(1)}, u32[]{:S(2)}, u32[]{:S(2)}) %collective-permute-start.4) | collective-permute-done | bytes 327712 | tf_op jit(solution)/shard_map/ppermute | solution.py:28
  63.0 0.7 slice.399
  63.7 0.7 slice.400
  65.0 0.7 slice.402
  65.7 0.7 slice.403
  66.3 0.7 slice.404
  67.0 0.7 slice.405
  67.7 0.8 slice.406
  68.6 0.7 slice.386
  69.2 0.7 slice.387
  69.9 0.7 slice.388
  71.4 0.8 constant_dynamic-update-slice_fusion.9
  72.2 0.8 constant_dynamic-update-slice_fusion.17
  73.0 0.8 constant_dynamic-update-slice_fusion.16
  73.7 0.8 constant_dynamic-update-slice_fusion.15
  74.5 0.8 constant_dynamic-update-slice_fusion.14
  75.3 0.8 constant_dynamic-update-slice_fusion.13
  76.0 0.8 constant_dynamic-update-slice_fusion.12
  76.8 0.8 constant_dynamic-update-slice_fusion.11
  77.6 0.8 constant_dynamic-update-slice_fusion.10
  78.6 0.8 constant_dynamic-update-slice_fusion.8
  79.4 0.8 constant_dynamic-update-slice_fusion.7
  80.7 1.4 copy.95
  82.1 2.9 concatenate.67
  85.0 3.6 pad_maximum_fusion
  88.7 1.3 dynamic-slice
  90.0 1.3 dynamic-slice.2
  91.3 1.3 dynamic-slice.4
  92.7 0.8 convolution_multiply_fusion.5
  93.5 132.0 %all-reduce.12.cloned.1.call-done = f32[4,16,8,1728]{3,2,1,0:T(8,128)} async-done(((f32[4,16,8,1728]{3,2,1,0:T(8,128)}), f32[4,16,8,1728]{3,2,1,0:T(8,128)}) %all-reduce.12.cloned.1.call-update) | async-done | bytes 3538960
  225.5 1.6 constant_dynamic-slice_fusion.1
  227.1 0.8 copy.71
  227.9 0.9 fusion.6
  228.8 1.4 fusion.8
  230.2 112.4 %all-reduce.14.cloned.1.call-done = f32[4,1,8,1728]{3,0,1,2:T(4,128)} async-done(((f32[4,1,8,1728]{3,0,1,2:T(4,128)}), f32[4,1,8,1728]{3,0,1,2:T(4,128)}) %all-reduce.14.cloned.1.call-update) | async-done | bytes 221200
  342.6 1.4 constant_dynamic-slice_fusion
  344.0 35.2 %all-reduce.8 = bf16[4,1,1,1728]{3,2,1,0:T(2,128)(2,1)S(1)} all-reduce(f32[4,1,1,1728]{3,2,1,0:T(1,128)S(1)} %copy.72), channel_id=4, replica_groups=mesh['dp'=4,'tm'=8,'height'=16] {'dp'}, use_global_device_ids=true, to_apply=%region_5.6.clone | all-reduce | flops 6912 | bytes 41472
  379.2 0.7 fusion.64
  379.9 48.0 %all_gather.6 = bf16[1,1,8,1728]{3,1,0,2:T(2,128)(2,1)S(1)} all-gather(bf16[1,1,1,1728]{3,1,0,2:T(2,128)(2,1)S(1)} %fusion.64), channel_id=1, replica_groups=mesh['dp'=4,'tm'=8,'height'=16] {'tm'}, dimensions={2}, use_global_device_ids=true | all-gather | bytes 31104 | tf_op jit(solution)/shard_map/all_gather | solution.py:171
  427.9 24.0 %all_gather.7 = bf16[1,16,8,1728]{3,2,0,1:T(8,128)(2,1)S(1)} all-gather(bf16[1,1,8,1728]{3,2,0,1:T(8,128)(2,1)S(1)} %copy.74), channel_id=1, replica_groups=mesh['dp'=4,'tm'=8,'height'=16] {'height'}, dimensions={1}, use_global_device_ids=true | all-gather | bytes 470016 | tf_op jit(solution)/shard_map/all_gather | solution.py:172
  451.9 1.0 reshape.211
  452.9 1.0 reshape.212
  (134 shorter events, 10.8 us)
Async XLA Ops:
  7.2 19.8 %copy-start = (bf16[1,2,4,128,128]{4,3,2,1,0:T(8,128)(2,1)S(1)}, bf16[1,2,4,128,128]{4,3,2,1,0:T(8,128)(2,1)}, u32[]{:S(2)}) copy-start(bf16[1,2,4,128,128]{4,3,2,1,0:T(8,128)(2,1)} %param.5) | copy-start | bytes 786436
  7.2 218.3 %all-reduce.12.cloned.1.call-start = ((), (), s32[]{:S(2)}) async-start(), calls=%async_computation | async-start | bytes 7340032
  8.1 18.8 %collective-permute-start = (bf16[2,1,128,128]{3,2,1,0:T(8,128)(2,1)S(1)}, bf16[2,1,128,128]{3,2,1,0:T(8,128)(2,1)S(1)}, u32[]{:S(2)}, u32[]{:S(2)}) collective-permute-start(bf16[2,1,128,128]{3,2,1,0:T(8,128)(2,1)S(1)} %get-tuple-element.17), channel_id=1, source_target_pairs={{0,1},{1,2},{2,3},{3,4},{4,5},{5,6},{6,7},{7,8},{8,9},{9,10},{10,1... | collective-permute-start | bytes 196616 | tf_op jit(solution)/shard_map/ppermute | solution.py:16
  11.6 15.3 %collective-permute-start.1 = (bf16[2,1,128,128]{3,2,1,0:T(8,128)(2,1)S(1)}, bf16[2,1,128,128]{3,2,1,0:T(8,128)(2,1)S(1)}, u32[]{:S(2)}, u32[]{:S(2)}) collective-permute-start(bf16[2,1,128,128]{3,2,1,0:T(8,128)(2,1)S(1)} %get-tuple-element.18), channel_id=1, source_target_pairs={{1,0},{2,1},{3,2},{4,3},{5,4},{6,5},{7,6},{8,7},{9,8},{10,9},{11,1... | collective-permute-start | bytes 196616 | tf_op jit(solution)/shard_map/ppermute | solution.py:18
  13.7 8.0 %collective-permute-start.5 = (bf16[1,1,64,128]{3,2,1,0:T(8,128)(2,1)S(1)}, bf16[1,1,64,128]{3,2,1,0:T(8,128)(2,1)S(1)}, u32[]{:S(2)}, u32[]{:S(2)}) collective-permute-start(bf16[1,1,64,128]{3,2,1,0:T(8,128)(2,1)S(1)} %slice.452), channel_id=1, source_target_pairs={{1,0},{2,1},{3,2},{4,3},{5,4},{6,5},{7,6},{8,7},{9,8},{10,9},{11,1... | collective-permute-start | bytes 49160 | tf_op jit(solution)/shard_map/ppermute | solution.py:28
  21.7 7.5 %collective-permute-start.6 = (bf16[1,3,64,128]{3,2,1,0:T(8,128)(2,1)S(1)}, bf16[1,3,64,128]{3,2,1,0:T(8,128)(2,1)S(1)}, u32[]{:S(2)}, u32[]{:S(2)}) collective-permute-start(bf16[1,3,64,128]{3,2,1,0:T(8,128)(2,1)S(1)} %pad_maximum_fusion.8), channel_id=1, source_target_pairs={{16,0},{32,16},{48,32},{64,48},{80,64},{96,80},{112,96},{17,1},{33... | collective-permute-start | bytes 147464 | tf_op jit(solution)/shard_map/ppermute | solution.py:28
  27.0 4.3 copy-start.1
  27.0 4.3 copy-start.4
  27.0 9.8 %collective-permute-start.2 = (bf16[2,6,128,128]{3,2,1,0:T(8,128)(2,1)S(1)}, bf16[2,6,128,128]{3,2,1,0:T(8,128)(2,1)S(1)}, u32[]{:S(2)}, u32[]{:S(2)}) collective-permute-start(bf16[2,6,128,128]{3,2,1,0:T(8,128)(2,1)S(1)} %pad_maximum_fusion.4), channel_id=1, source_target_pairs={{0,16},{16,32},{32,48},{48,64},{64,80},{80,96},{96,112},{1,17},{17... | collective-permute-start | bytes 1179656 | tf_op jit(solution)/shard_map/ppermute | solution.py:28
  43.9 8.6 %collective-permute-start.3 = (bf16[2,1,128,128]{3,2,1,0:T(8,128)(2,1)S(1)}, bf16[2,1,128,128]{3,2,1,0:T(8,128)(2,1)S(1)}, u32[]{:S(2)}, u32[]{:S(2)}) collective-permute-start(bf16[2,1,128,128]{3,2,1,0:T(8,128)(2,1)S(1)} %slice.447), channel_id=1, source_target_pairs={{0,1},{1,2},{2,3},{3,4},{4,5},{5,6},{6,7},{7,8},{8,9},{9,10},{10,1... | collective-permute-start | bytes 196616 | tf_op jit(solution)/shard_map/ppermute | solution.py:28
  50.6 6.6 %copy-start.3 = (bf16[1,1,2,64,128]{4,3,2,1,0:T(8,128)(2,1)S(1)}, bf16[1,1,2,64,128]{4,3,2,1,0:T(8,128)(2,1)}, u32[]{:S(2)}) copy-start(bf16[1,1,2,64,128]{4,3,2,1,0:T(8,128)(2,1)} %param.9) | copy-start | bytes 98308
  53.9 9.0 %collective-permute-start.4 = (bf16[2,5,128,128]{3,2,1,0:T(8,128)(2,1)S(1)}, bf16[2,5,128,128]{3,2,1,0:T(8,128)(2,1)S(1)}, u32[]{:S(2)}, u32[]{:S(2)}) collective-permute-start(bf16[2,5,128,128]{3,2,1,0:T(8,128)(2,1)S(1)} %pad_maximum_fusion.3), channel_id=1, source_target_pairs={{0,16},{16,32},{32,48},{48,64},{64,80},{80,96},{96,112},{1,17},{17... | collective-permute-start | bytes 983048 | tf_op jit(solution)/shard_map/ppermute | solution.py:28
  88.6 3.9 copy-start.2
  88.7 253.9 %all-reduce.14.cloned.1.call-start = ((), (), s32[]{:S(2)}) async-start(), calls=%async_computation.1 | async-start | bytes 458752
Sparse Core Ops, SparseCore 0:
  88.8 136.6 all-reduce.11
  228.4 114.1 all-reduce.13
where the time goes:
time: 462 us; the launch traced here: 461 us
  waiting for transfers between devices  253 us (55%)
  blocking collectives  107 us (23%)
  local copies, waits for them, and re-layouts  43.2 us (9%)
  starting transfers between devices  21.8 us (5%)
  between operations  16.9 us (4%)
  matrix products  10 us (2%)
  other arithmetic  8.16 us (2%)
    unnamed x4, waiting for transfers between devices  244 us
    all_gather x1, blocking collectives, body(): piece = lax.all_gather(piece, 'tm', axis=2, tiled=True)  48 us
    unnamed x1, blocking collectives  35.2 us
    all_gather x1, blocking collectives, body(): gathered = lax.all_gather(piece, 'height', axis=1, tiled=True).reshape(-1)  24 us
    unnamed x66, local copies, waits for them, and re-layouts  17 us
    ppermute x5, starting transfers between devices, shifted(): lax.ppermute(value, axis, [(source, source + steps) for source in range(l...  17 us
    slice x27, local copies, waits for them, and re-layouts, unfold(): padded[:, tap_row:tap_row + stride * (out_rows - 1) + 1:stride, tap_col:t...  9.5 us
  transfers between devices with their start and end apart: 9, of which 4 were waited for; matrix products, arithmetic and copies ran while one was open for 4% of the time, Pallas kernels for 0%

commit v1 on v0

--- a/solution.py
+++ b/solution.py
@@ -109,6 +109,32 @@
 
 
 def body(clips, frame_counts, conv_first, conv_down, out_cotangent):
+
+    def _get_skins(axis_key, content):
+        plain = lax.psum(1, axis_name=axis_key)
+        mat_out = lax.axis_index(axis_key)
+        heard, frame_out, row_out = (plain, mat_out, content.shape[1])
+        val2 = jnp.zeros(
+            [i0 * heard if pp == 1 else i0 for pp, i0 in enumerate(content.shape)], content.dtype
+        )
+        upper = lax.dynamic_update_slice_in_dim(val2, content, frame_out * row_out, axis=1)
+        f_now = block_next = content
+        for h in range(1, heard // 2 + 1):
+            f_now = lax.ppermute(
+                f_now, axis_key, perm=[(pp, (pp + 1) % heard) for pp in range(heard)]
+            )
+            upper = lax.dynamic_update_slice_in_dim(
+                upper, f_now, (frame_out - h) % heard * row_out, axis=1
+            )
+            if 2 * h < heard:
+                block_next = lax.ppermute(
+                    block_next, axis_key, [(pp, (pp - 1) % heard) for pp in range(heard)]
+                )
+                upper = lax.dynamic_update_slice_in_dim(
+                    upper, block_next, (frame_out + h) % heard * row_out, axis=1
+                )
+        return upper
+
     frames_dev = clips.shape[1]
     rows_dev = clips.shape[2]
     columns_all = clips.shape[3]
@@ -169,7 +195,7 @@
     piece = lax.psum_scatter(piece, "dp", scatter_dimension=0, tiled=True)
     piece = piece.astype(jnp.bfloat16)
     piece = lax.all_gather(piece, "tm", axis=2, tiled=True)
-    gathered = lax.all_gather(piece, "height", axis=1, tiled=True).reshape(-1)
+    gathered = _get_skins("height", piece).reshape(-1)
     half = gathered.shape[0] // 2
     kernel_shape = (3, 3, 3, share, conv_first.shape[-1])
     summed_first = gathered[:half].reshape(kernel_shape)

time: 462 us -> 514 us (1.11)
  starting transfers between devices: 21.8 us -> 87.7 us
  blocking collectives: 107 us -> 83.2 us
  waiting for transfers between devices: 253 us -> 262 us
    ppermute x0 -> x15, starting transfers between devices: none -> 66 us  [the longest x7 49.2 us: _get_skins(): lax.ppermute(block_next, axis_key, [(pp, (pp - 1) % heard) for pp in rang...]
    all_gather x1 -> x0, blocking collectives: 24 us -> none  [body(): gathered = lax.all_gather(piece, 'height', axis=1, tiled=True).reshape(-1)]
    ppermute x0 -> x15, waiting for transfers between devices: none -> 8.88 us  [the longest x8 8.87 us: _get_skins(): lax.ppermute(f_now, axis_key, perm=[(pp, (pp + 1) % heard) for pp in rang...]
  transfers between devices with their start and end apart: 9 -> 24, of which waited for: 4 -> 12; matrix products, arithmetic and copies ran while one was open for 4% -> 4% of each run, Pallas kernels for 0% -> 0%
where the time goes in v1:
time: 514 us; the launch traced here: 512 us
  waiting for transfers between devices  262 us (51%)
  starting transfers between devices  87.7 us (17%)
  blocking collectives  83.2 us (16%)
  local copies, waits for them, and re-layouts  43.3 us (8%)
  between operations  17.5 us (3%)
  matrix products  10 us (2%)
  other arithmetic  8.14 us (2%)
    unnamed x4, waiting for transfers between devices  244 us
    ppermute x7, starting transfers between devices, _get_skins(): lax.ppermute(block_next, axis_key, [(pp, (pp - 1) % heard) for pp in rang...  49.2 us
    all_gather x1, blocking collectives, body(): piece = lax.all_gather(piece, 'tm', axis=2, tiled=True)  48 us
    unnamed x1, blocking collectives  35.2 us
    unnamed x66, local copies, waits for them, and re-layouts  16.9 us
    ppermute x5, starting transfers between devices, shifted(): lax.ppermute(value, axis, [(source, source + steps) for source in range(l...  16.8 us
    ppermute x8, starting transfers between devices, _get_skins(): lax.ppermute(f_now, axis_key, perm=[(pp, (pp + 1) % heard) for pp in rang...  16.8 us
  transfers between devices with their start and end apart: 24, of which 12 were waited for; matrix products, arithmetic and copies ran while one was open for 4% of the time, Pallas kernels for 0%

profile of v1, /device:TPU:32, one launch (start us, length us, event | category | flops | bytes accessed | tf_op | source)
XLA Modules:
  0.0 512.0 jit_solution(456662591205294138)
XLA Ops:
  7.2 0.9 fusion.92
  8.1 3.5 collective-permute-start
  11.6 1.3 collective-permute-start.1
  12.9 0.8 fusion.60
  13.7 1.3 collective-permute-start.5
  15.0 0.8 reduce-window_clone.1
  16.9 1.3 fusion.89
  21.8 5.2 %collective-permute-start.6 = (bf16[1,3,64,128]{3,2,1,0:T(8,128)(2,1)S(1)}, bf16[1,3,64,128]{3,2,1,0:T(8,128)(2,1)S(1)}, u32[]{:S(2)}, u32[]{:S(2)}) collective-permute-start(bf16[1,3,64,128]{3,2,1,0:T(8,128)(2,1)S(1)} %pad_maximum_fusion.8), channel_id=1, source_target_pairs={{16,0},{32,16},{48,32},{64,48},{80,64},{96,80},{112,96},{17,1},{33... | collective-permute-start | bytes 147464 | tf_op jit(solution)/shard_map/ppermute | solution.py:28
  27.1 1.9 collective-permute-start.2
  29.2 1.3 multiply_bitcast_fusion.1
  33.0 3.8 collective-permute-done.2
  37.8 0.8 convolution_multiply_fusion.1
  39.5 0.8 fusion.1
  40.3 0.9 fusion.10
  41.3 0.9 convolution_bitcast_fusion.5
  42.1 0.9 convolution_bitcast_fusion.4
  43.0 0.9 convolution_bitcast_fusion.3
  43.9 5.2 %collective-permute-start.3 = (bf16[2,1,128,128]{3,2,1,0:T(8,128)(2,1)S(1)}, bf16[2,1,128,128]{3,2,1,0:T(8,128)(2,1)S(1)}, u32[]{:S(2)}, u32[]{:S(2)}) collective-permute-start(bf16[2,1,128,128]{3,2,1,0:T(8,128)(2,1)S(1)} %slice.447), channel_id=1, source_target_pairs={{0,1},{1,2},{2,3},{3,4},{4,5},{5,6},{6,7},{7,8},{8,9},{9,10},{10,1... | collective-permute-start | bytes 196616 | tf_op jit(solution)/shard_map/ppermute | solution.py:28
  49.2 1.4 copy.142
  50.6 1.9 concatenate.66
  53.8 3.2 collective-permute-start.4
  57.5 5.3 %collective-permute-done.4 = bf16[2,5,128,128]{3,2,1,0:T(8,128)(2,1)S(1)} collective-permute-done((bf16[2,5,128,128]{3,2,1,0:T(8,128)(2,1)S(1)}, bf16[2,5,128,128]{3,2,1,0:T(8,128)(2,1)S(1)}, u32[]{:S(2)}, u32[]{:S(2)}) %collective-permute-start.4) | collective-permute-done | bytes 327712 | tf_op jit(solution)/shard_map/ppermute | solution.py:28
  67.7 0.8 slice.406
  72.1 0.8 constant_dynamic-update-slice_fusion.17
  72.9 0.8 constant_dynamic-update-slice_fusion.16
  73.7 0.8 constant_dynamic-update-slice_fusion.15
  74.5 0.8 constant_dynamic-update-slice_fusion.14
  75.2 0.8 constant_dynamic-update-slice_fusion.13
  76.0 0.8 constant_dynamic-update-slice_fusion.12
  78.6 0.8 constant_dynamic-update-slice_fusion.8
  80.7 1.4 copy.141
  82.1 2.9 concatenate.67
  84.9 3.6 pad_maximum_fusion
  88.9 1.3 dynamic-slice
  90.1 1.3 dynamic-slice.2
  91.4 1.3 dynamic-slice.4
  92.8 0.8 convolution_multiply_fusion.5
  93.6 131.8 %all-reduce.12.cloned.1.call-done = f32[4,16,8,1728]{3,2,1,0:T(8,128)} async-done(((f32[4,16,8,1728]{3,2,1,0:T(8,128)}), f32[4,16,8,1728]{3,2,1,0:T(8,128)}) %all-reduce.12.cloned.1.call-update) | async-done | bytes 3538960
  225.4 1.6 constant_dynamic-slice_fusion.1
  227.0 0.8 copy.86
  227.8 0.9 fusion.6
  228.6 1.4 fusion.8
  230.1 112.4 %all-reduce.14.cloned.1.call-done = f32[4,1,8,1728]{3,0,1,2:T(4,128)} async-done(((f32[4,1,8,1728]{3,0,1,2:T(4,128)}), f32[4,1,8,1728]{3,0,1,2:T(4,128)}) %all-reduce.14.cloned.1.call-update) | async-done | bytes 221200
  342.5 1.4 constant_dynamic-slice_fusion
  343.9 35.2 %all-reduce.8 = bf16[4,1,1,1728]{3,2,1,0:T(2,128)(2,1)S(1)} all-reduce(f32[4,1,1,1728]{3,2,1,0:T(1,128)S(1)} %copy.87), channel_id=4, replica_groups=mesh['dp'=4,'tm'=8,'height'=16] {'dp'}, use_global_device_ids=true, to_apply=%region_5.6.clone | all-reduce | flops 6912 | bytes 41472
  379.8 48.0 %all_gather.3 = bf16[1,1,8,1728]{3,1,0,2:T(2,128)(2,1)S(1)} all-gather(bf16[1,1,1,1728]{3,1,0,2:T(2,128)(2,1)S(1)} %fusion.64), channel_id=1, replica_groups=mesh['dp'=4,'tm'=8,'height'=16] {'tm'}, dimensions={2}, use_global_device_ids=true | all-gather | bytes 31104 | tf_op jit(solution)/shard_map/all_gather | solution.py:197
  427.8 3.4 collective-permute-start.7
  431.2 5.8 %collective-permute-start.8 = (bf16[1,1,8,1728]{3,1,0,2:T(2,128)(2,1)S(1)}, bf16[1,1,8,1728]{3,1,0,2:T(2,128)(2,1)S(1)}, u32[]{:S(2)}, u32[]{:S(2)}) collective-permute-start(bf16[1,1,8,1728]{3,1,0,2:T(2,128)(2,1)S(1)} %all_gather.3), channel_id=1, source_target_pairs={{0,15},{1,0},{2,1},{3,2},{4,3},{5,4},{6,5},{7,6},{8,7},{9,8},{10,9... | collective-permute-start | bytes 82952 | tf_op jit(solution)/shard_map/ppermute | solution.py:130
  437.2 1.9 collective-permute-start.9
  439.1 7.2 %collective-permute-start.10 = (bf16[1,1,8,1728]{3,1,0,2:T(2,128)(2,1)S(1)}, bf16[1,1,8,1728]{3,1,0,2:T(2,128)(2,1)S(1)}, u32[]{:S(2)}, u32[]{:S(2)}) collective-permute-start(bf16[1,1,8,1728]{3,1,0,2:T(2,128)(2,1)S(1)} %collective-permute-done.8), channel_id=1, source_target_pairs={{0,15},{1,0},{2,1},{3,2},{4,3},{5,4},{6,5},{7,6},{8,7},{9,8},{10,9... | collective-permute-start | bytes 82952 | tf_op jit(solution)/shard_map/ppermute | solution.py:130
  446.6 1.9 collective-permute-start.11
  448.5 7.2 %collective-permute-start.12 = (bf16[1,1,8,1728]{3,1,0,2:T(2,128)(2,1)S(1)}, bf16[1,1,8,1728]{3,1,0,2:T(2,128)(2,1)S(1)}, u32[]{:S(2)}, u32[]{:S(2)}) collective-permute-start(bf16[1,1,8,1728]{3,1,0,2:T(2,128)(2,1)S(1)} %collective-permute-done.10), channel_id=1, source_target_pairs={{0,15},{1,0},{2,1},{3,2},{4,3},{5,4},{6,5},{7,6},{8,7},{9,8},{10,9... | collective-permute-start | bytes 82952 | tf_op jit(solution)/shard_map/ppermute | solution.py:130
  455.9 1.9 collective-permute-start.13
  457.9 7.2 %collective-permute-start.14 = (bf16[1,1,8,1728]{3,1,0,2:T(2,128)(2,1)S(1)}, bf16[1,1,8,1728]{3,1,0,2:T(2,128)(2,1)S(1)}, u32[]{:S(2)}, u32[]{:S(2)}) collective-permute-start(bf16[1,1,8,1728]{3,1,0,2:T(2,128)(2,1)S(1)} %collective-permute-done.12), channel_id=1, source_target_pairs={{0,15},{1,0},{2,1},{3,2},{4,3},{5,4},{6,5},{7,6},{8,7},{9,8},{10,9... | collective-permute-start | bytes 82952 | tf_op jit(solution)/shard_map/ppermute | solution.py:130
  465.3 1.9 collective-permute-start.15
  467.2 7.2 %collective-permute-start.16 = (bf16[1,1,8,1728]{3,1,0,2:T(2,128)(2,1)S(1)}, bf16[1,1,8,1728]{3,1,0,2:T(2,128)(2,1)S(1)}, u32[]{:S(2)}, u32[]{:S(2)}) collective-permute-start(bf16[1,1,8,1728]{3,1,0,2:T(2,128)(2,1)S(1)} %collective-permute-done.14), channel_id=1, source_target_pairs={{0,15},{1,0},{2,1},{3,2},{4,3},{5,4},{6,5},{7,6},{8,7},{9,8},{10,9... | collective-permute-start | bytes 82952 | tf_op jit(solution)/shard_map/ppermute | solution.py:130
  474.7 1.9 collective-permute-start.17
  476.6 7.2 %collective-permute-start.18 = (bf16[1,1,8,1728]{3,1,0,2:T(2,128)(2,1)S(1)}, bf16[1,1,8,1728]{3,1,0,2:T(2,128)(2,1)S(1)}, u32[]{:S(2)}, u32[]{:S(2)}) collective-permute-start(bf16[1,1,8,1728]{3,1,0,2:T(2,128)(2,1)S(1)} %collective-permute-done.16), channel_id=1, source_target_pairs={{0,15},{1,0},{2,1},{3,2},{4,3},{5,4},{6,5},{7,6},{8,7},{9,8},{10,9... | collective-permute-start | bytes 82952 | tf_op jit(solution)/shard_map/ppermute | solution.py:130
  484.4 1.9 collective-permute-start.19
  486.3 7.2 %collective-permute-start.20 = (bf16[1,1,8,1728]{3,1,0,2:T(2,128)(2,1)S(1)}, bf16[1,1,8,1728]{3,1,0,2:T(2,128)(2,1)S(1)}, u32[]{:S(2)}, u32[]{:S(2)}) collective-permute-start(bf16[1,1,8,1728]{3,1,0,2:T(2,128)(2,1)S(1)} %collective-permute-done.18), channel_id=1, source_target_pairs={{0,15},{1,0},{2,1},{3,2},{4,3},{5,4},{6,5},{7,6},{8,7},{9,8},{10,9... | collective-permute-start | bytes 82952 | tf_op jit(solution)/shard_map/ppermute | solution.py:130
  493.8 1.9 collective-permute-start.21
  495.7 7.4 %collective-permute-done.21 = bf16[1,1,8,1728]{3,1,0,2:T(2,128)(2,1)S(1)} collective-permute-done((bf16[1,1,8,1728]{3,1,0,2:T(2,128)(2,1)S(1)}, bf16[1,1,8,1728]{3,1,0,2:T(2,128)(2,1)S(1)}, u32[]{:S(2)}, u32[]{:S(2)}) %collective-permute-start.21) | collective-permute-done | bytes 27680 | tf_op jit(solution)/shard_map/ppermute | solution.py:123
  503.2 1.0 reshape.211
  504.2 1.0 reshape.212
  (179 shorter events, 22.9 us)
Async XLA Ops:
  7.2 19.9 %copy-start = (bf16[1,2,4,128,128]{4,3,2,1,0:T(8,128)(2,1)S(1)}, bf16[1,2,4,128,128]{4,3,2,1,0:T(8,128)(2,1)}, u32[]{:S(2)}) copy-start(bf16[1,2,4,128,128]{4,3,2,1,0:T(8,128)(2,1)} %param.5) | copy-start | bytes 786436
  7.2 218.2 %all-reduce.12.cloned.1.call-start = ((), (), s32[]{:S(2)}) async-start(), calls=%async_computation | async-start | bytes 7340032
  8.1 18.9 %collective-permute-start = (bf16[2,1,128,128]{3,2,1,0:T(8,128)(2,1)S(1)}, bf16[2,1,128,128]{3,2,1,0:T(8,128)(2,1)S(1)}, u32[]{:S(2)}, u32[]{:S(2)}) collective-permute-start(bf16[2,1,128,128]{3,2,1,0:T(8,128)(2,1)S(1)} %get-tuple-element.17), channel_id=1, source_target_pairs={{0,1},{1,2},{2,3},{3,4},{4,5},{5,6},{6,7},{7,8},{8,9},{9,10},{10,1... | collective-permute-start | bytes 196616 | tf_op jit(solution)/shard_map/ppermute | solution.py:16
  11.6 15.4 %collective-permute-start.1 = (bf16[2,1,128,128]{3,2,1,0:T(8,128)(2,1)S(1)}, bf16[2,1,128,128]{3,2,1,0:T(8,128)(2,1)S(1)}, u32[]{:S(2)}, u32[]{:S(2)}) collective-permute-start(bf16[2,1,128,128]{3,2,1,0:T(8,128)(2,1)S(1)} %get-tuple-element.18), channel_id=1, source_target_pairs={{1,0},{2,1},{3,2},{4,3},{5,4},{6,5},{7,6},{8,7},{9,8},{10,9},{11,1... | collective-permute-start | bytes 196616 | tf_op jit(solution)/shard_map/ppermute | solution.py:18
  13.7 8.1 %collective-permute-start.5 = (bf16[1,1,64,128]{3,2,1,0:T(8,128)(2,1)S(1)}, bf16[1,1,64,128]{3,2,1,0:T(8,128)(2,1)S(1)}, u32[]{:S(2)}, u32[]{:S(2)}) collective-permute-start(bf16[1,1,64,128]{3,2,1,0:T(8,128)(2,1)S(1)} %slice.452), channel_id=1, source_target_pairs={{1,0},{2,1},{3,2},{4,3},{5,4},{6,5},{7,6},{8,7},{9,8},{10,9},{11,1... | collective-permute-start | bytes 49160 | tf_op jit(solution)/shard_map/ppermute | solution.py:28
  16.9 14.0 %copy-start.1 = (bf16[3,3,3,128,128]{4,3,2,1,0:T(8,128)(2,1)S(1)}, bf16[3,3,3,128,128]{4,3,2,1,0:T(8,128)(2,1)}, u32[]{:S(2)}) copy-start(bf16[3,3,3,128,128]{4,3,2,1,0:T(8,128)(2,1)} %param.8) | copy-start | bytes 2654212
  16.9 14.0 %copy-start.4 = (pred[8,18]{0,1:T(8,128)(4,1)S(1)}, pred[8,18]{0,1:T(8,128)(4,1)}, u32[]{:S(2)}) copy-start(pred[8,18]{0,1:T(8,128)(4,1)} %constant.154) | copy-start | bytes 436
  21.8 7.3 %collective-permute-start.6 = (bf16[1,3,64,128]{3,2,1,0:T(8,128)(2,1)S(1)}, bf16[1,3,64,128]{3,2,1,0:T(8,128)(2,1)S(1)}, u32[]{:S(2)}, u32[]{:S(2)}) collective-permute-start(bf16[1,3,64,128]{3,2,1,0:T(8,128)(2,1)S(1)} %pad_maximum_fusion.8), channel_id=1, source_target_pairs={{16,0},{32,16},{48,32},{64,48},{80,64},{96,80},{112,96},{17,1},{33... | collective-permute-start | bytes 147464 | tf_op jit(solution)/shard_map/ppermute | solution.py:28
  27.1 9.7 %collective-permute-start.2 = (bf16[2,6,128,128]{3,2,1,0:T(8,128)(2,1)S(1)}, bf16[2,6,128,128]{3,2,1,0:T(8,128)(2,1)S(1)}, u32[]{:S(2)}, u32[]{:S(2)}) collective-permute-start(bf16[2,6,128,128]{3,2,1,0:T(8,128)(2,1)S(1)} %pad_maximum_fusion.4), channel_id=1, source_target_pairs={{0,16},{16,32},{32,48},{48,64},{64,80},{80,96},{96,112},{1,17},{17... | collective-permute-start | bytes 1179656 | tf_op jit(solution)/shard_map/ppermute | solution.py:28
  43.9 8.6 %collective-permute-start.3 = (bf16[2,1,128,128]{3,2,1,0:T(8,128)(2,1)S(1)}, bf16[2,1,128,128]{3,2,1,0:T(8,128)(2,1)S(1)}, u32[]{:S(2)}, u32[]{:S(2)}) collective-permute-start(bf16[2,1,128,128]{3,2,1,0:T(8,128)(2,1)S(1)} %slice.447), channel_id=1, source_target_pairs={{0,1},{1,2},{2,3},{3,4},{4,5},{5,6},{6,7},{7,8},{8,9},{9,10},{10,1... | collective-permute-start | bytes 196616 | tf_op jit(solution)/shard_map/ppermute | solution.py:28
  50.6 6.6 %copy-start.3 = (bf16[1,1,2,64,128]{4,3,2,1,0:T(8,128)(2,1)S(1)}, bf16[1,1,2,64,128]{4,3,2,1,0:T(8,128)(2,1)}, u32[]{:S(2)}) copy-start(bf16[1,1,2,64,128]{4,3,2,1,0:T(8,128)(2,1)} %param.9) | copy-start | bytes 98308
  53.8 9.0 %collective-permute-start.4 = (bf16[2,5,128,128]{3,2,1,0:T(8,128)(2,1)S(1)}, bf16[2,5,128,128]{3,2,1,0:T(8,128)(2,1)S(1)}, u32[]{:S(2)}, u32[]{:S(2)}) collective-permute-start(bf16[2,5,128,128]{3,2,1,0:T(8,128)(2,1)S(1)} %pad_maximum_fusion.3), channel_id=1, source_target_pairs={{0,16},{16,32},{32,48},{48,64},{64,80},{80,96},{96,112},{1,17},{17... | collective-permute-start | bytes 983048 | tf_op jit(solution)/shard_map/ppermute | solution.py:28
  88.6 4.1 copy-start.2
  88.6 253.9 %all-reduce.14.cloned.1.call-start = ((), (), s32[]{:S(2)}) async-start(), calls=%async_computation.1 | async-start | bytes 458752
  427.8 9.4 %collective-permute-start.7 = (bf16[1,1,8,1728]{3,1,0,2:T(2,128)(2,1)S(1)}, bf16[1,1,8,1728]{3,1,0,2:T(2,128)(2,1)S(1)}, u32[]{:S(2)}, u32[]{:S(2)}) collective-permute-start(bf16[1,1,8,1728]{3,1,0,2:T(2,128)(2,1)S(1)} %all_gather.3), channel_id=1, source_target_pairs={{0,1},{1,2},{2,3},{3,4},{4,5},{5,6},{6,7},{7,8},{8,9},{9,10},{10,1... | collective-permute-start | bytes 82952 | tf_op jit(solution)/shard_map/ppermute | solution.py:123
  431.2 7.9 %collective-permute-start.8 = (bf16[1,1,8,1728]{3,1,0,2:T(2,128)(2,1)S(1)}, bf16[1,1,8,1728]{3,1,0,2:T(2,128)(2,1)S(1)}, u32[]{:S(2)}, u32[]{:S(2)}) collective-permute-start(bf16[1,1,8,1728]{3,1,0,2:T(2,128)(2,1)S(1)} %all_gather.3), channel_id=1, source_target_pairs={{0,15},{1,0},{2,1},{3,2},{4,3},{5,4},{6,5},{7,6},{8,7},{9,8},{10,9... | collective-permute-start | bytes 82952 | tf_op jit(solution)/shard_map/ppermute | solution.py:130
  437.2 9.4 %collective-permute-start.9 = (bf16[1,1,8,1728]{3,1,0,2:T(2,128)(2,1)S(1)}, bf16[1,1,8,1728]{3,1,0,2:T(2,128)(2,1)S(1)}, u32[]{:S(2)}, u32[]{:S(2)}) collective-permute-start(bf16[1,1,8,1728]{3,1,0,2:T(2,128)(2,1)S(1)} %collective-permute-done.7), channel_id=1, source_target_pairs={{0,1},{1,2},{2,3},{3,4},{4,5},{5,6},{6,7},{7,8},{8,9},{9,10},{10,1... | collective-permute-start | bytes 82952 | tf_op jit(solution)/shard_map/ppermute | solution.py:123
  439.1 9.4 %collective-permute-start.10 = (bf16[1,1,8,1728]{3,1,0,2:T(2,128)(2,1)S(1)}, bf16[1,1,8,1728]{3,1,0,2:T(2,128)(2,1)S(1)}, u32[]{:S(2)}, u32[]{:S(2)}) collective-permute-start(bf16[1,1,8,1728]{3,1,0,2:T(2,128)(2,1)S(1)} %collective-permute-done.8), channel_id=1, source_target_pairs={{0,15},{1,0},{2,1},{3,2},{4,3},{5,4},{6,5},{7,6},{8,7},{9,8},{10,9... | collective-permute-start | bytes 82952 | tf_op jit(solution)/shard_map/ppermute | solution.py:130
  446.6 9.4 %collective-permute-start.11 = (bf16[1,1,8,1728]{3,1,0,2:T(2,128)(2,1)S(1)}, bf16[1,1,8,1728]{3,1,0,2:T(2,128)(2,1)S(1)}, u32[]{:S(2)}, u32[]{:S(2)}) collective-permute-start(bf16[1,1,8,1728]{3,1,0,2:T(2,128)(2,1)S(1)} %collective-permute-done.9), channel_id=1, source_target_pairs={{0,1},{1,2},{2,3},{3,4},{4,5},{5,6},{6,7},{7,8},{8,9},{9,10},{10,1... | collective-permute-start | bytes 82952 | tf_op jit(solution)/shard_map/ppermute | solution.py:123
  448.5 9.4 %collective-permute-start.12 = (bf16[1,1,8,1728]{3,1,0,2:T(2,128)(2,1)S(1)}, bf16[1,1,8,1728]{3,1,0,2:T(2,128)(2,1)S(1)}, u32[]{:S(2)}, u32[]{:S(2)}) collective-permute-start(bf16[1,1,8,1728]{3,1,0,2:T(2,128)(2,1)S(1)} %collective-permute-done.10), channel_id=1, source_target_pairs={{0,15},{1,0},{2,1},{3,2},{4,3},{5,4},{6,5},{7,6},{8,7},{9,8},{10,9... | collective-permute-start | bytes 82952 | tf_op jit(solution)/shard_map/ppermute | solution.py:130
  455.9 9.4 %collective-permute-start.13 = (bf16[1,1,8,1728]{3,1,0,2:T(2,128)(2,1)S(1)}, bf16[1,1,8,1728]{3,1,0,2:T(2,128)(2,1)S(1)}, u32[]{:S(2)}, u32[]{:S(2)}) collective-permute-start(bf16[1,1,8,1728]{3,1,0,2:T(2,128)(2,1)S(1)} %collective-permute-done.11), channel_id=1, source_target_pairs={{0,1},{1,2},{2,3},{3,4},{4,5},{5,6},{6,7},{7,8},{8,9},{9,10},{10,1... | collective-permute-start | bytes 82952 | tf_op jit(solution)/shard_map/ppermute | solution.py:123
  457.9 9.4 %collective-permute-start.14 = (bf16[1,1,8,1728]{3,1,0,2:T(2,128)(2,1)S(1)}, bf16[1,1,8,1728]{3,1,0,2:T(2,128)(2,1)S(1)}, u32[]{:S(2)}, u32[]{:S(2)}) collective-permute-start(bf16[1,1,8,1728]{3,1,0,2:T(2,128)(2,1)S(1)} %collective-permute-done.12), channel_id=1, source_target_pairs={{0,15},{1,0},{2,1},{3,2},{4,3},{5,4},{6,5},{7,6},{8,7},{9,8},{10,9... | collective-permute-start | bytes 82952 | tf_op jit(solution)/shard_map/ppermute | solution.py:130
  465.3 9.4 %collective-permute-start.15 = (bf16[1,1,8,1728]{3,1,0,2:T(2,128)(2,1)S(1)}, bf16[1,1,8,1728]{3,1,0,2:T(2,128)(2,1)S(1)}, u32[]{:S(2)}, u32[]{:S(2)}) collective-permute-start(bf16[1,1,8,1728]{3,1,0,2:T(2,128)(2,1)S(1)} %collective-permute-done.13), channel_id=1, source_target_pairs={{0,1},{1,2},{2,3},{3,4},{4,5},{5,6},{6,7},{7,8},{8,9},{9,10},{10,1... | collective-permute-start | bytes 82952 | tf_op jit(solution)/shard_map/ppermute | solution.py:123
  467.2 9.4 %collective-permute-start.16 = (bf16[1,1,8,1728]{3,1,0,2:T(2,128)(2,1)S(1)}, bf16[1,1,8,1728]{3,1,0,2:T(2,128)(2,1)S(1)}, u32[]{:S(2)}, u32[]{:S(2)}) collective-permute-start(bf16[1,1,8,1728]{3,1,0,2:T(2,128)(2,1)S(1)} %collective-permute-done.14), channel_id=1, source_target_pairs={{0,15},{1,0},{2,1},{3,2},{4,3},{5,4},{6,5},{7,6},{8,7},{9,8},{10,9... | collective-permute-start | bytes 82952 | tf_op jit(solution)/shard_map/ppermute | solution.py:130
  474.7 9.7 %collective-permute-start.17 = (bf16[1,1,8,1728]{3,1,0,2:T(2,128)(2,1)S(1)}, bf16[1,1,8,1728]{3,1,0,2:T(2,128)(2,1)S(1)}, u32[]{:S(2)}, u32[]{:S(2)}) collective-permute-start(bf16[1,1,8,1728]{3,1,0,2:T(2,128)(2,1)S(1)} %collective-permute-done.15), channel_id=1, source_target_pairs={{0,1},{1,2},{2,3},{3,4},{4,5},{5,6},{6,7},{7,8},{8,9},{9,10},{10,1... | collective-permute-start | bytes 82952 | tf_op jit(solution)/shard_map/ppermute | solution.py:123
  476.6 9.7 %collective-permute-start.18 = (bf16[1,1,8,1728]{3,1,0,2:T(2,128)(2,1)S(1)}, bf16[1,1,8,1728]{3,1,0,2:T(2,128)(2,1)S(1)}, u32[]{:S(2)}, u32[]{:S(2)}) collective-permute-start(bf16[1,1,8,1728]{3,1,0,2:T(2,128)(2,1)S(1)} %collective-permute-done.16), channel_id=1, source_target_pairs={{0,15},{1,0},{2,1},{3,2},{4,3},{5,4},{6,5},{7,6},{8,7},{9,8},{10,9... | collective-permute-start | bytes 82952 | tf_op jit(solution)/shard_map/ppermute | solution.py:130
  484.4 9.4 %collective-permute-start.19 = (bf16[1,1,8,1728]{3,1,0,2:T(2,128)(2,1)S(1)}, bf16[1,1,8,1728]{3,1,0,2:T(2,128)(2,1)S(1)}, u32[]{:S(2)}, u32[]{:S(2)}) collective-permute-start(bf16[1,1,8,1728]{3,1,0,2:T(2,128)(2,1)S(1)} %collective-permute-done.17), channel_id=1, source_target_pairs={{0,1},{1,2},{2,3},{3,4},{4,5},{5,6},{6,7},{7,8},{8,9},{9,10},{10,1... | collective-permute-start | bytes 82952 | tf_op jit(solution)/shard_map/ppermute | solution.py:123
  486.3 9.4 %collective-permute-start.20 = (bf16[1,1,8,1728]{3,1,0,2:T(2,128)(2,1)S(1)}, bf16[1,1,8,1728]{3,1,0,2:T(2,128)(2,1)S(1)}, u32[]{:S(2)}, u32[]{:S(2)}) collective-permute-start(bf16[1,1,8,1728]{3,1,0,2:T(2,128)(2,1)S(1)} %collective-permute-done.18), channel_id=1, source_target_pairs={{0,15},{1,0},{2,1},{3,2},{4,3},{5,4},{6,5},{7,6},{8,7},{9,8},{10,9... | collective-permute-start | bytes 82952 | tf_op jit(solution)/shard_map/ppermute | solution.py:130
  493.8 9.4 %collective-permute-start.21 = (bf16[1,1,8,1728]{3,1,0,2:T(2,128)(2,1)S(1)}, bf16[1,1,8,1728]{3,1,0,2:T(2,128)(2,1)S(1)}, u32[]{:S(2)}, u32[]{:S(2)}) collective-permute-start(bf16[1,1,8,1728]{3,1,0,2:T(2,128)(2,1)S(1)} %collective-permute-done.19), channel_id=1, source_target_pairs={{0,1},{1,2},{2,3},{3,4},{4,5},{5,6},{6,7},{7,8},{8,9},{9,10},{10,1... | collective-permute-start | bytes 82952 | tf_op jit(solution)/shard_map/ppermute | solution.py:123
Sparse Core Ops, SparseCore 0:
  88.7 136.6 all-reduce.11
  228.3 114.1 all-reduce.13
